TPU v7x, 256 devices: a whole 4x4x8 slice. The times are simulated.
256 devices in a mesh: view: 16 (over z, y_hi), row: 16 (over x, y_lo, core).
Axes of the slice: x: 4, y: 4 (y_hi: 2, y_lo: 2; y = y_hi * 2 + y_lo), z: 8, core: 2. Of those that a mesh axis runs over, the one named last changes fastest.
Arguments:
- latent: bfloat16 [1, 16, 32, 72, 1280], P(None, 'view', 'row'), may hold values from -30 to 30
- gn_gain: float32 [1280], replicated, may hold values from 0.25 to 1.75
- gn_bias: float32 [1280], replicated, may hold values from -3 to 3
- cam_idx: int32 [1, 16], P(None, 'view'), may hold values from 0 to 63
- noise_idx: int32 [1], replicated, may hold values from 0 to 999
- cam_table: bfloat16 [64, 2560], replicated, may hold values from -2 to 2
- noise_table: bfloat16 [1000, 2560], replicated, may hold values from -2 to 2
- conv_w: bfloat16 [3, 3, 1280, 1280], P(None, None, None, 'row'), may hold values from -0.0546875 to 0.0546875
- conv_bias: float32 [1280], replicated, may hold values from -3 to 3
- ln_gain: float32 [1280], replicated, may hold values from 0.25 to 1.75
- attn_in: bfloat16 [3, 1280, 1280], P(None, None, 'view'), may hold values from -0.15625 to 0.15625
- attn_out: bfloat16 [1280, 1280], P('view'), may hold values from -0.15625 to 0.15625
- head_scale: float32 [20], replicated, may hold values from 0.4 to 135
Outputs:
- block_out: bfloat16 [1, 16, 32, 72, 1280], P(None, 'view', 'row')
All inputs are finite; a program needn't handle non-finite values.
Results may differ from a plain program's by a relative error of at most 0.02.
Values may be sent and summed in bfloat16 or wider, within the bound.
No kernel may reach another device: no remote copies, remote signals or barrier semaphores. Data moves between devices by JAX's collectives and lax.ppermute only.
A program may use at most 192 MiB of HBM per device.

v0:
```python
import math
import jax
import jax.numpy as jnp
from jax import lax
from jax.sharding import PartitionSpec as P

GROUPS = 32
epsilon = 1e-05


def attend(query, key_block, value, head_scale):
    view_count = query.shape[0]
    item_count = query.shape[2]
    channels = query.shape[3]
    head_count = head_scale.shape[0]
    head_size = channels // head_count
    query_heads = query.reshape(view_count, item_count, head_count, head_size)
    key_heads = key_block.reshape(view_count, item_count, head_count, head_size)
    value_heads = value.reshape(view_count, item_count, head_count, head_size)
    scores = jnp.einsum(
        "vihd,uihd->ihvu", query_heads, key_heads, preferred_element_type=jnp.float32
    )
    scores = scores * (head_scale / math.sqrt(head_size))[None, :, None, None]
    peak_score = jnp.max(scores, axis=-1, keepdims=True)
    exp_scores = jnp.exp(scores - peak_score)
    soft_weights = (exp_scores / jnp.sum(exp_scores, axis=-1, keepdims=True)).astype(jnp.bfloat16)
    mixed = jnp.einsum(
        "ihvu,uihd->vihd", soft_weights, value_heads, preferred_element_type=jnp.float32
    )
    return mixed.astype(jnp.bfloat16).reshape(view_count, 1, item_count, channels)


def send_back(mixed):
    return lax.all_to_all(mixed, "view", split_axis=0, concat_axis=1, tiled=True)


def local(
    latent,
    gn_gain,
    gn_bias,
    cam_idx,
    noise_idx,
    cam_table,
    noise_table,
    conv_w,
    conv_bias,
    ln_gain,
    attn_in,
    attn_out,
    head_scale,
):
    samples, local_views, local_rows, local_cols, channels = latent.shape
    width_out = ln_gain.shape[0]
    out_part = conv_w.shape[-1]
    whole = lax.all_gather(latent, ROW, axis=2, tiled=True)
    whole, attn_in, attn_out = lax.optimization_barrier((whole, attn_in, attn_out))
    core = lax.axis_index("core")
    half_in = attn_in.shape[1] // 2
    half_out = attn_out.shape[1] // 2
    in_half = lax.dynamic_slice_in_dim(attn_in, core * half_in, half_in, axis=1)
    in_half = lax.all_gather(in_half, "view", axis=0, tiled=False)
    out_half = lax.dynamic_slice_in_dim(attn_out, core * half_out, half_out, axis=1)
    all_rows = whole.shape[2]
    x_float = whole.astype(jnp.float32)
    grouped = x_float.reshape(
        samples, local_views, all_rows, local_cols, GROUPS, channels // GROUPS
    )
    average = jnp.mean(grouped, axis=(2, 3, 5), keepdims=True)
    centred = grouped - average
    variance = jnp.mean(centred * centred, axis=(2, 3, 5), keepdims=True)
    normed = (centred * lax.rsqrt(variance + epsilon)).reshape(x_float.shape)
    cam_hot = (cam_idx[:, :, None] == jnp.arange(cam_table.shape[0], dtype=jnp.int32)).astype(
        jnp.bfloat16
    )
    cam_film = jnp.einsum("svn,nc->svc", cam_hot, cam_table, preferred_element_type=jnp.float32)
    noise_hot = (noise_idx[:, None] == jnp.arange(noise_table.shape[0], dtype=jnp.int32)).astype(
        jnp.bfloat16
    )
    noise_film = jnp.dot(noise_hot, noise_table, preferred_element_type=jnp.float32)
    film_rows = cam_film + noise_film[:, None, :]
    film_scale = film_rows[:, :, None, None, :channels]
    film_shift = film_rows[:, :, None, None, channels:]
    hidden = (normed * gn_gain + gn_bias) * (1.0 + film_scale) + film_shift
    activated = jax.nn.silu(hidden).astype(jnp.bfloat16)
    conv_out = lax.conv_general_dilated(
        activated.reshape(samples * local_views, all_rows, local_cols, channels),
        conv_w,
        window_strides=(1, 1),
        padding=((1, 1), (1, 1)),
        dimension_numbers=("NHWC", "HWIO", "NHWC"),
        preferred_element_type=jnp.float32,
    ).reshape(samples, local_views, all_rows, local_cols, out_part)
    me = lax.axis_index("chip") * lax.axis_size("core") + core
    bias_part = lax.dynamic_slice_in_dim(conv_bias, me * out_part, out_part)
    latent_part = lax.dynamic_slice_in_dim(whole, me * out_part, out_part, axis=4)
    resid_part = (latent_part.astype(jnp.float32) + conv_out + bias_part).astype(jnp.bfloat16)
    in_half, resid_part = lax.optimization_barrier((in_half, resid_part))
    weights_in = lax.all_gather(in_half, "core", axis=0, tiled=False)
    resid_out = lax.all_to_all(resid_part, ROW, split_axis=2, concat_axis=4, tiled=True)
    resid_float = resid_out.astype(jnp.float32)
    middle = jnp.mean(resid_float, axis=-1, keepdims=True)
    spread_y = jnp.mean((resid_float - middle) ** 2, axis=-1, keepdims=True)
    normed_y = ((resid_float - middle) * lax.rsqrt(spread_y + epsilon) * ln_gain).astype(
        jnp.bfloat16
    )
    view_devices = lax.axis_size("view")
    per_device = samples * local_rows * local_cols // view_devices
    pixel_major = jnp.moveaxis(normed_y, 1, 0).reshape(
        local_views, view_devices, per_device, width_out
    )
    flat_block = pixel_major.reshape(-1, 2, width_out // 2)
    triple_in = jnp.einsum(
        "pkc,kjmcd->mpjd", flat_block, weights_in, preferred_element_type=jnp.float32
    ).astype(jnp.bfloat16)
    triple_in = triple_in.reshape((3,) + pixel_major.shape)
    out_half, triple_in = lax.optimization_barrier((out_half, triple_in))
    out_half = lax.all_gather(out_half, "view", axis=0, tiled=True)
    triple_in = lax.all_to_all(triple_in, "view", split_axis=2, concat_axis=1, tiled=True)
    mixed = send_back(attend(triple_in[0], triple_in[1], triple_in[2], head_scale))
    out_half, mixed = lax.optimization_barrier((out_half, mixed))
    weights_out = lax.all_gather(out_half, "core", axis=0, tiled=False)
    mixed = jnp.moveaxis(
        mixed.reshape(local_views, samples, local_rows, local_cols, width_out), 0, 1
    )
    flat_mixed = mixed.reshape(-1, width_out)
    projected = jnp.einsum(
        "pc,kcd->pkd", flat_mixed, weights_out, preferred_element_type=jnp.float32
    )
    return (resid_float + projected.reshape(resid_float.shape)).astype(jnp.bfloat16)


ROW = ("chip", "core")


def solution(mesh):
    cores = 2
    split = jax.sharding.Mesh(
        mesh.devices.reshape(mesh.shape["view"], mesh.shape["row"] // cores, cores),
        ("view", "chip", "core"),
    )
    placed = (
        P(None, "view", ROW, None, None),
        P(),
        P(),
        P(None, "view"),
        P(),
        P(),
        P(),
        P(None, None, None, ROW),
        P(),
        P(),
        P(None, None, "view"),
        P("view", None),
        P(),
    )
    return jax.shard_map(
        local,
        mesh=split,
        in_specs=placed,
        out_specs=P(None, "view", ROW, None, None),
        check_vma=False,
    )
```

profile of v0, /device:TPU:1, one launch (start us, length us, event | category | flops | bytes accessed | tf_op | source)
XLA Modules:
  0.0 350.6 jit_solution(10321813126953900763)
XLA Ops:
  7.3 49.7 %all-gather.9.cloned.1.call-done = bf16[1,1,32,72,1280]{4,3,1,0,2:T(8,128)(2,1)} async-done(((bf16[1,1,2,72,1280]{4,3,1,0,2:T(8,128)(2,1)}), bf16[1,1,32,72,1280]{4,3,1,0,2:T(8,128)(2,1)}) %all-gather.9.cloned.1.call-update) | async-done | bytes 5898256 | tf_op jit(solution)/shard_map/all_gather | solution.py:55
  57.0 1.7 constant_dynamic-slice_fusion.1
  61.2 3.4 convolution_reduce_fusion
  65.2 1.3 dynamic_slice.14
  66.5 1.3 fusion.43
  67.9 6.8 %copy.79 = bf16[1,1,32,72,1280]{4,2,3,1,0:T(8,128)(2,1)} copy(bf16[1,1,32,72,1280]{4,3,1,0,2:T(8,128)(2,1)} %all-gather.9.cloned.1.call-done) | data formatting | bytes 11796480 | tf_op jit(solution)/shard_map/optimization_barrier | solution.py:56
  75.9 4.5 %fusion.4 = f32[1280]{0:T(1024)S(1)} fusion(f32[1280]{0:T(1024)S(1)} %sub.48, bf16[1,1,32,72,1280]{4,3,1,0,2:T(8,128)(2,1)} %all-gather.9.cloned.1.call-done), kind=kLoop, calls=%fused_computation.7 | loop fusion | flops 11795200 | bytes 5908480 | tf_op jit(solution)/shard_map/reduce_sum | solution.py:70
  80.8 8.7 %fusion.16 = bf16[32,1,72,1280]{3,0,2,1:T(8,128)(2,1)S(1)} fusion(f32[1280]{0:T(1024)S(1)} %copy-done.4, f32[1280]{0:T(1024)S(1)} %copy-done.3, f32[1280]{0:T(1024)S(1)} %copy-done.6, f32[1280]{0:T(1024)S(1)} %copy-done.7, f32[1280]{0:T(1024)S(1)} %mul.96, f32[1280]{0:T(1024)S(1)} %sub.48, bf16[1,1,32,72,1280]{4,3,1,0,2:T(8,128)(2,1)} %all-gather.9.cloned.1.call-done), kind=kLoop, calls=%fused_computation.19 | loop fusion | flops 35389440 | bytes 11827200 | tf_op jit(solution)/shard_map/reshape | solution.py:86
  90.3 3.6 %copy.82 = bf16[32,1,8,10,1280]{4,2,3,0,1:T(8,128)(2,1)S(1)} copy(bf16[32,1,8,10,1280]{4,0,3,2,1:T(8,128)(2,1)S(1)} %bitcast.78) | data formatting | bytes 13107200 | tf_op jit(solution)/shard_map/conv_general_dilated | solution.py:85
  94.3 17.0 %fusion.23 = f32[32,8,10,80]{3,1,2,0:T(8,128)S(1)} fusion(bf16[3,3,1280,80]{2,3,1,0:T(8,128)(2,1)S(1)} %copy-done, bf16[32,1,7,2,1280]{4,2,3,0,1:T(8,128)(2,1)S(1)} %slice.28, bf16[32,1,8,10,1280]{4,2,3,0,1:T(8,128)(2,1)S(1)} %copy.82, pred[8,10]{0,1:T(8,128)(4,1)S(1)} %copy-done.10), kind=kOutput, calls=%fused_computation.31 | convolution fusion | flops 4644085760 | bytes 10362960 | tf_op jit(solution)/shard_map/conv_general_dilated | solution.py:85
  111.7 1.6 fusion.29
  113.4 48.8 %all-gather.13.cloned.1.call-done = bf16[48,640,80]{1,2,0:T(8,128)(2,1)} async-done(((bf16[3,640,80]{1,2,0:T(8,128)(2,1)}), bf16[48,640,80]{1,2,0:T(8,128)(2,1)}) %all-gather.13.cloned.1.call-update) | async-done | bytes 4915216 | tf_op jit(solution)/shard_map/all_gather | solution.py:61
  163.2 7.9 %all-to-all-start = ((bf16[1,1,32,72,80]{4,3,1,0,2:T(8,128)(2,1)}), bf16[1,1,32,72,80]{4,3,1,0,2:T(8,128)(2,1)S(1)}, u32[]{:S(2)}, u32[]{:S(2)}) async-start(bf16[1,1,32,72,80]{4,3,1,0,2:T(8,128)(2,1)} %copy.84), calls=%async_computation | async-start | bytes 1179648 | tf_op jit(solution)/shard_map/all_to_all | solution.py:99
  171.8 9.4 %all-to-all-done = bf16[1,1,32,72,80]{4,3,1,0,2:T(8,128)(2,1)S(1)} async-done(((bf16[1,1,32,72,80]{4,3,1,0,2:T(8,128)(2,1)}), bf16[1,1,32,72,80]{4,3,1,0,2:T(8,128)(2,1)S(1)}, u32[]{:S(2)}, u32[]{:S(2)}) %all-to-all-start) | async-done | bytes 368672 | tf_op jit(solution)/shard_map/all_to_all | solution.py:99
  182.2 2.0 multiply_reduce_fusion
  185.3 6.5 %all-gather.15.cloned.1.call-done = bf16[32,3,640,80]{2,3,1,0:T(8,128)(2,1)} async-done(((bf16[16,3,640,80]{2,3,1,0:T(8,128)(2,1)}), bf16[32,3,640,80]{2,3,1,0:T(8,128)(2,1)}) %all-gather.15.cloned.1.call-update) | async-done | bytes 9830416 | tf_op jit(solution)/shard_map/all_gather | solution.py:98
  191.8 8.2 %fusion.38 = bf16[16,3,80,144,1]{2,3,1,0,4:T(8,128)(2,1)S(1)} fusion(bf16[2,16,3,640,80]{3,4,2,1,0:T(8,128)(2,1)} %bitcast.91, f32[144,2,640]{2,1,0:T(2,128)S(1)} %reshape.199, f32[2,640]{1,0:T(2,128)S(1)} %mul.106, f32[144]{0:T(256)S(1)} %rsqrt.21, f32[144]{0:T(256)S(1)} %div.35), kind=kOutput, calls=%fused_computation.53 | convolution fusion | flops 1416314880 | bytes 11679872 | tf_op jit(solution)/shard_map/pkc,kjmcd->mpjd/dot_general | solution.py:112
  200.1 1.7 copy.88
  201.8 5.7 %reshape.189 = bf16[3,1,16,9,1280]{4,0,3,2,1:T(4,128)(2,1)} reshape(bf16[3,144,16,80]{3,2,0,1:T(8,128)(2,1)} %copy.88) | data formatting | bytes 2211840 | tf_op jit(solution)/shard_map/reshape | solution.py:115
  207.5 9.0 %all-to-all-start.1 = ((bf16[3,1,16,9,1280]{4,0,3,1,2:T(4,128)(2,1)}), bf16[3,1,16,9,1280]{4,0,3,1,2:T(4,128)(2,1)S(1)}, u32[]{:S(2)}, u32[]{:S(2)}) async-start(bf16[3,1,16,9,1280]{4,0,3,1,2:T(4,128)(2,1)} %bitcast.83), calls=%async_computation.1 | async-start | bytes 2949120 | tf_op jit(solution)/shard_map/all_to_all | solution.py:118
  217.1 36.4 %all-to-all-done.1 = bf16[3,1,16,9,1280]{4,0,3,1,2:T(4,128)(2,1)S(1)} async-done(((bf16[3,1,16,9,1280]{4,0,3,1,2:T(4,128)(2,1)}), bf16[3,1,16,9,1280]{4,0,3,1,2:T(4,128)(2,1)S(1)}, u32[]{:S(2)}, u32[]{:S(2)}) %all-to-all-start.1) | async-done | bytes 1105952 | tf_op jit(solution)/shard_map/all_to_all | solution.py:118
  253.5 6.4 %slice_reduce_fusion.2 = (bf16[16,9,1280]{2,1,0:T(8,128)(2,1)S(1)}, bf16[16,9,1280]{2,1,0:T(8,128)(2,1)}, bf16[16,9,1280]{2,1,0:T(8,128)(2,1)}) fusion(bf16[3,1,16,9,1280]{4,0,3,1,2:T(4,128)(2,1)S(1)} %all-to-all-done.1), kind=kLoop, calls=%fused_computation.43 | loop fusion | bytes 2211840 | tf_op jit(solution)/shard_map/slice | solution.py:119
  259.9 1.8 reshape.221
  261.7 2.5 reshape.222
  264.2 1.6 reshape.220
  265.7 3.2 fusion.56
  268.9 2.1 fusion.26
  271.8 29.6 %all_to_all.30 = bf16[16,1,9,1280]{3,2,1,0:T(8,128)(2,1)S(1)} all-to-all(bf16[16,1,9,1280]{3,2,1,0:T(8,128)(2,1)S(1)} %reshape.223), channel_id=1, replica_groups=mesh['view'=16,'chip'=8,'core'=2] {'view'}, dimensions={0} | all-to-all | bytes 737280 | tf_op jit(solution)/shard_map/all_to_all | solution.py:34
  301.4 10.8 %all-gather.11.cloned.1.call-done = bf16[1280,640]{1,0:T(8,128)(2,1)} async-done(((bf16[80,640]{1,0:T(8,128)(2,1)}), bf16[1280,640]{1,0:T(8,128)(2,1)}) %all-gather.11.cloned.1.call-update) | async-done | bytes 1638416 | tf_op jit(solution)/shard_map/all_gather | solution.py:117
  313.0 21.1 %all-gather.17.cloned.1.call-done = bf16[2560,640]{1,0:T(8,128)(2,1)} async-done(((bf16[1280,640]{1,0:T(8,128)(2,1)}), bf16[2560,640]{1,0:T(8,128)(2,1)}) %all-gather.17.cloned.1.call-update) | async-done | bytes 3276816 | tf_op jit(solution)/shard_map/all_gather | solution.py:121
  334.2 5.7 %copy.99 = bf16[2,1280,640]{1,2,0:T(8,128)(2,1)} copy(bf16[2,1280,640]{2,1,0:T(8,128)(2,1)} %bitcast.88) | data formatting | bytes 6553600 | tf_op jit(solution)/shard_map/all_gather | solution.py:121
  339.9 3.9 %fusion.19 = bf16[1,1,2,72,1280]{4,3,2,1,0:T(8,128)(2,1)} fusion(f32[2,72,1280]{2,1,0:T(8,128)S(1)} %reshape.198, bf16[2,72,1280]{2,1,0:T(8,128)(2,1)S(1)} %dot_general.29, bf16[1280,1280,1]{1,0,2:T(8,128)(2,1)} %bitcast.79), kind=kOutput, calls=%fused_computation.24 | convolution fusion | flops 472227840 | bytes 4751360 | tf_op jit(solution)/shard_map/pc,kcd->pkd/dot_general | solution.py:126
  (73 shorter events, 11.8 us)
Async XLA Ops:
  6.5 87.7 %copy-start = (bf16[3,3,1280,80]{2,3,1,0:T(8,128)(2,1)S(1)}, bf16[3,3,1280,80]{2,3,1,0:T(8,128)(2,1)}, u32[]{:S(2)}) copy-start(bf16[3,3,1280,80]{2,3,1,0:T(8,128)(2,1)} %param.20) | copy-start | bytes 5529604
  6.5 50.4 %all-gather.9.cloned.1.call-start = ((), (), s32[]{:S(2)}) async-start(), calls=%async_computation.3 | async-start | bytes 6266880 | tf_op jit(solution)/shard_map/all_gather | solution.py:55
  7.3 154.9 %all-gather.13.cloned.1.call-start = ((), (), s32[]{:S(2)}) async-start(), calls=%async_computation.5 | async-start | bytes 5222400 | tf_op jit(solution)/shard_map/all_gather | solution.py:61
  58.7 133.1 %all-gather.15.cloned.1.call-start = ((), (), s32[]{:S(2)}) async-start(), calls=%async_computation.6 | async-start | bytes 14745600 | tf_op jit(solution)/shard_map/all_gather | solution.py:98
  61.2 13.4 %slice-start = ((s8[5898240]{0:T(1024)(128)(4,1)}), s8[1703936]{0:T(1024)(128)(4,1)S(1)}, s32[]{:S(2)}) async-start(s8[5898240]{0:T(1024)(128)(4,1)} %bitcast.76), calls=%async_computation.8 | async-start | bytes 3407872
  67.9 6.8 %slice-start.1 = ((s8[5898240]{0:T(1024)(128)(4,1)}), s8[4194304]{0:T(1024)(128)(4,1)S(1)}, s32[]{:S(2)}) async-start(s8[5898240]{0:T(1024)(128)(4,1)} %bitcast.76), calls=%async_computation.9 | async-start | bytes 8388608
  75.5 5.3 %copy-start.3 = (f32[1280]{0:T(1024)S(1)}, f32[1280]{0:T(1024)}, u32[]{:S(2)}) copy-start(f32[1280]{0:T(1024)} %get-tuple-element.26) | copy-start | bytes 15364
  75.5 5.3 %copy-start.4 = (f32[1280]{0:T(1024)S(1)}, f32[1280]{0:T(1024)}, u32[]{:S(2)}) copy-start(f32[1280]{0:T(1024)} %get-tuple-element.27) | copy-start | bytes 15364
  75.5 5.3 %copy-start.6 = (f32[1280]{0:T(1024)S(1)}, f32[1280]{0:T(1024)}, u32[]{:S(2)}) copy-start(f32[1280]{0:T(1024)} %param.15) | copy-start | bytes 15364
  75.5 5.3 %copy-start.7 = (f32[1280]{0:T(1024)S(1)}, f32[1280]{0:T(1024)}, u32[]{:S(2)}) copy-start(f32[1280]{0:T(1024)} %param.14) | copy-start | bytes 15364
  90.3 4.0 %copy-start.10 = (pred[8,10]{0,1:T(8,128)(4,1)S(1)}, pred[8,10]{0,1:T(8,128)(4,1)}, u32[]{:S(2)}) copy-start(pred[8,10]{0,1:T(8,128)(4,1)} %constant.46) | copy-start | bytes 244
  94.3 17.4 %copy-start.8 = (f32[80]{0:T(128)S(1)}, f32[80]{0:T(128)}, u32[]{:S(2)}) copy-start(f32[80]{0:T(128)} %dynamic_slice.14) | copy-start | bytes 964
  111.7 59.4 %copy-start.5 = (f32[1280]{0:T(1024)S(1)}, f32[1280]{0:T(1024)}, u32[]{:S(2)}) copy-start(f32[1280]{0:T(1024)} %param.22) | copy-start | bytes 15364
  111.7 59.5 %copy-start.2 = (bf16[80,1280]{1,0:T(8,128)(2,1)S(1)}, bf16[80,1280]{1,0:T(8,128)(2,1)}, u32[]{:S(2)}) copy-start(bf16[80,1280]{1,0:T(8,128)(2,1)} %param.24) | copy-start | bytes 614404
  163.2 17.9 %all-to-all-start = ((bf16[1,1,32,72,80]{4,3,1,0,2:T(8,128)(2,1)}), bf16[1,1,32,72,80]{4,3,1,0,2:T(8,128)(2,1)S(1)}, u32[]{:S(2)}, u32[]{:S(2)}) async-start(bf16[1,1,32,72,80]{4,3,1,0,2:T(8,128)(2,1)} %copy.84), calls=%async_computation | async-start | bytes 1179648 | tf_op jit(solution)/shard_map/all_to_all | solution.py:99
  200.1 17.0 %copy-start.9 = (f32[20]{0:T(128)S(1)}, f32[20]{0:T(128)}, u32[]{:S(2)}) copy-start(f32[20]{0:T(128)} %param.25) | copy-start | bytes 244
  207.5 46.1 %all-to-all-start.1 = ((bf16[3,1,16,9,1280]{4,0,3,1,2:T(4,128)(2,1)}), bf16[3,1,16,9,1280]{4,0,3,1,2:T(4,128)(2,1)S(1)}, u32[]{:S(2)}, u32[]{:S(2)}) async-start(bf16[3,1,16,9,1280]{4,0,3,1,2:T(4,128)(2,1)} %bitcast.83), calls=%async_computation.1 | async-start | bytes 2949120 | tf_op jit(solution)/shard_map/all_to_all | solution.py:118
  216.5 95.8 %all-gather.11.cloned.1.call-start = ((), (), s32[]{:S(2)}) async-start(), calls=%async_computation.4 | async-start | bytes 1740800 | tf_op jit(solution)/shard_map/all_gather | solution.py:117
  217.1 117.1 %all-gather.17.cloned.1.call-start = ((), (), s32[]{:S(2)}) async-start(), calls=%async_computation.7 | async-start | bytes 4915200 | tf_op jit(solution)/shard_map/all_gather | solution.py:121
  334.2 9.6 %copy-start.1 = (bf16[3,3,1280,80]{2,3,1,0:T(8,128)(2,1)S(1)}, bf16[3,3,1280,80]{2,3,1,0:T(8,128)(2,1)}, u32[]{:S(2)}) copy-start(bf16[3,3,1280,80]{2,3,1,0:T(8,128)(2,1)} %param.20) | copy-start | bytes 5529604
Sparse Core Ops, SparseCore 0:
  9.2 47.7 all-gather.8
  59.6 102.5 all-gather.12
  164.0 27.7 all-gather.14
  219.6 92.6 all-gather.10
  313.9 20.1 all-gather.16
where the time goes:
time: 357 us; the launch traced here: 351 us
  waiting for transfers between devices  184 us (52%)
  local copies, waits for them, and re-layouts  46 us (13%)
  matrix products  38.8 us (11%)
  blocking collectives  29.6 us (8%)
  other arithmetic  20 us (6%)
  starting transfers between devices  17.1 us (5%)
  between operations  15.1 us (4%)
    all_gather x1, waiting for transfers between devices, local(): whole = lax.all_gather(latent, ROW, axis=2, tiled=True)  49.7 us
    all_gather x1, waiting for transfers between devices, local(): in_half = lax.all_gather(in_half, 'view', axis=0, tiled=False)  48.8 us
    all_to_all x1, waiting for transfers between devices, local(): lax.all_to_all(triple_in, 'view', split_axis=2, concat_axis=1, tiled=True)  36.4 us
    all_to_all x1, blocking collectives, send_back(): lax.all_to_all(mixed, 'view', split_axis=0, concat_axis=1, tiled=True)  29.6 us
    all_gather x1, waiting for transfers between devices, local(): weights_out = lax.all_gather(out_half, 'core', axis=0, tiled=False)  21.1 us
    conv_general_dilated x1, matrix products, local(): lax.conv_general_dilated(activated.reshape(samples * local_views, all_row...  17 us
    all_gather x1, waiting for transfers between devices, local(): out_half = lax.all_gather(out_half, 'view', axis=0, tiled=True)  10.8 us
    all_to_all x1, waiting for transfers between devices, local(): lax.all_to_all(resid_part, ROW, split_axis=2, concat_axis=4, tiled=True)  9.36 us
  transfers between devices with their start and end apart: 7, of which 7 were waited for; matrix products, arithmetic and copies ran while one was open for 22% of the time, Pallas kernels for 0%

commit v1 on v0

--- a/solution.py
+++ b/solution.py
@@ -114,7 +114,8 @@
     ).astype(jnp.bfloat16)
     triple_in = triple_in.reshape((3,) + pixel_major.shape)
     out_half, triple_in = lax.optimization_barrier((out_half, triple_in))
-    out_half = lax.all_gather(out_half, "view", axis=0, tiled=True)
+    sent = jnp.stack([out_half] * lax.axis_size("view"))
+    out_half = jnp.concatenate(lax.all_to_all(sent, "view", 0, 0), axis=0)
     triple_in = lax.all_to_all(triple_in, "view", split_axis=2, concat_axis=1, tiled=True)
     mixed = send_back(attend(triple_in[0], triple_in[1], triple_in[2], head_scale))
     out_half, mixed = lax.optimization_barrier((out_half, mixed))

time: 357 us -> 381 us (1.067)
  blocking collectives: 29.6 us -> 71.6 us
  waiting for transfers between devices: 184 us -> 166 us
    all_to_all x0 -> x1, blocking collectives: none -> 44.1 us  [local(): out_half = jnp.concatenate(lax.all_to_all(sent, 'view', 0, 0), axis=0)]
    all_gather x1 -> x0, waiting for transfers between devices: 10.8 us -> none  [local(): out_half = lax.all_gather(out_half, 'view', axis=0, tiled=True)]
    all_gather x1, waiting for transfers between devices: 21.1 us -> 14.8 us  [local(): weights_out = lax.all_gather(out_half, 'core', axis=0, tiled=False)]
    dot_general x1 -> x2, local copies, waits for them, and re-layouts: 0.17 us -> 5.89 us  [local(): jnp.einsum('pc,kcd->pkd', flat_mixed, weights_out, preferred_element_type...]
    all_gather x1 -> x0, local copies, waits for them, and re-layouts: 5.72 us -> none  [local(): weights_out = lax.all_gather(out_half, 'core', axis=0, tiled=False)]
  transfers between devices with their start and end apart: 7 -> 6, of which waited for: 7 -> 6; matrix products, arithmetic and copies ran while one was open for 22% -> 16% of each run, Pallas kernels for 0% -> 0%
where the time goes in v1:
time: 381 us; the launch traced here: 374 us
  waiting for transfers between devices  166 us (44%)
  blocking collectives  71.6 us (19%)
  local copies, waits for them, and re-layouts  45.5 us (12%)
  matrix products  38.8 us (10%)
  other arithmetic  20 us (5%)
  starting transfers between devices  17 us (4%)
  between operations  15.1 us (4%)
    all_gather x1, waiting for transfers between devices, local(): whole = lax.all_gather(latent, ROW, axis=2, tiled=True)  49.7 us
    all_gather x1, waiting for transfers between devices, local(): in_half = lax.all_gather(in_half, 'view', axis=0, tiled=False)  48.8 us
    all_to_all x1, blocking collectives, local(): out_half = jnp.concatenate(lax.all_to_all(sent, 'view', 0, 0), axis=0)  44.1 us
    all_to_all x1, waiting for transfers between devices, local(): lax.all_to_all(triple_in, 'view', split_axis=2, concat_axis=1, tiled=True)  35.6 us
    all_to_all x1, blocking collectives, send_back(): lax.all_to_all(mixed, 'view', split_axis=0, concat_axis=1, tiled=True)  27.5 us
    conv_general_dilated x1, matrix products, local(): lax.conv_general_dilated(activated.reshape(samples * local_views, all_row...  17 us
    all_gather x1, waiting for transfers between devices, local(): weights_out = lax.all_gather(out_half, 'core', axis=0, tiled=False)  14.8 us
    all_to_all x1, waiting for transfers between devices, local(): lax.all_to_all(resid_part, ROW, split_axis=2, concat_axis=4, tiled=True)  9.99 us
  transfers between devices with their start and end apart: 6, of which 6 were waited for; matrix products, arithmetic and copies ran while one was open for 16% of the time, Pallas kernels for 0%

profile of v1, /device:TPU:1, one launch (start us, length us, event | category | flops | bytes accessed | tf_op | source)
XLA Modules:
  0.0 374.2 jit_solution(3337870117527379704)
XLA Ops:
  7.3 49.7 %all-gather.8.cloned.1.call-done = bf16[1,1,32,72,1280]{4,3,1,0,2:T(8,128)(2,1)} async-done(((bf16[1,1,2,72,1280]{4,3,1,0,2:T(8,128)(2,1)}), bf16[1,1,32,72,1280]{4,3,1,0,2:T(8,128)(2,1)}) %all-gather.8.cloned.1.call-update) | async-done | bytes 5898256 | tf_op jit(solution)/shard_map/all_gather | solution.py:55
  57.0 1.7 constant_dynamic-slice_fusion.1
  61.2 3.4 convolution_reduce_fusion
  65.2 1.3 dynamic_slice.14
  66.5 1.3 fusion.43
  67.9 6.8 %copy.78 = bf16[1,1,32,72,1280]{4,2,3,1,0:T(8,128)(2,1)} copy(bf16[1,1,32,72,1280]{4,3,1,0,2:T(8,128)(2,1)} %all-gather.8.cloned.1.call-done) | data formatting | bytes 11796480 | tf_op jit(solution)/shard_map/optimization_barrier | solution.py:56
  75.9 4.5 %fusion.4 = f32[1280]{0:T(1024)S(1)} fusion(f32[1280]{0:T(1024)S(1)} %sub.48, bf16[1,1,32,72,1280]{4,3,1,0,2:T(8,128)(2,1)} %all-gather.8.cloned.1.call-done), kind=kLoop, calls=%fused_computation.7 | loop fusion | flops 11795200 | bytes 5908480 | tf_op jit(solution)/shard_map/reduce_sum | solution.py:70
  80.8 8.7 %fusion.16 = bf16[32,1,72,1280]{3,0,2,1:T(8,128)(2,1)S(1)} fusion(f32[1280]{0:T(1024)S(1)} %copy-done.4, f32[1280]{0:T(1024)S(1)} %copy-done.3, f32[1280]{0:T(1024)S(1)} %copy-done.6, f32[1280]{0:T(1024)S(1)} %copy-done.7, f32[1280]{0:T(1024)S(1)} %mul.96, f32[1280]{0:T(1024)S(1)} %sub.48, bf16[1,1,32,72,1280]{4,3,1,0,2:T(8,128)(2,1)} %all-gather.8.cloned.1.call-done), kind=kLoop, calls=%fused_computation.19 | loop fusion | flops 35389440 | bytes 11827200 | tf_op jit(solution)/shard_map/reshape | solution.py:86
  90.3 3.6 copy.81
  94.3 17.0 %fusion.23 = f32[32,8,10,80]{3,1,2,0:T(8,128)S(1)} fusion(bf16[3,3,1280,80]{2,3,1,0:T(8,128)(2,1)S(1)} %copy-done, bf16[32,1,7,2,1280]{4,2,3,0,1:T(8,128)(2,1)S(1)} %slice.28, bf16[32,1,8,10,1280]{4,2,3,0,1:T(8,128)(2,1)S(1)} %copy.81, pred[8,10]{0,1:T(8,128)(4,1)S(1)} %copy-done.10), kind=kOutput, calls=%fused_computation.31 | convolution fusion | flops 4644085760 | bytes 10362960 | tf_op jit(solution)/shard_map/conv_general_dilated | solution.py:85
  111.7 1.6 fusion.29
  113.4 48.8 %all-gather.10.cloned.1.call-done = bf16[48,640,80]{1,2,0:T(8,128)(2,1)} async-done(((bf16[3,640,80]{1,2,0:T(8,128)(2,1)}), bf16[48,640,80]{1,2,0:T(8,128)(2,1)}) %all-gather.10.cloned.1.call-update) | async-done | bytes 4915216 | tf_op jit(solution)/shard_map/all_gather | solution.py:61
  163.2 7.9 %all-to-all-start = ((bf16[1,1,32,72,80]{4,3,1,0,2:T(8,128)(2,1)}), bf16[1,1,32,72,80]{4,3,1,0,2:T(8,128)(2,1)S(1)}, u32[]{:S(2)}, u32[]{:S(2)}) async-start(bf16[1,1,32,72,80]{4,3,1,0,2:T(8,128)(2,1)} %copy.83), calls=%async_computation | async-start | bytes 1179648 | tf_op jit(solution)/shard_map/all_to_all | solution.py:99
  171.2 10.0 %all-to-all-done = bf16[1,1,32,72,80]{4,3,1,0,2:T(8,128)(2,1)S(1)} async-done(((bf16[1,1,32,72,80]{4,3,1,0,2:T(8,128)(2,1)}), bf16[1,1,32,72,80]{4,3,1,0,2:T(8,128)(2,1)S(1)}, u32[]{:S(2)}, u32[]{:S(2)}) %all-to-all-start) | async-done | bytes 368672 | tf_op jit(solution)/shard_map/all_to_all | solution.py:99
  182.2 2.0 multiply_reduce_fusion
  185.3 6.5 %all-gather.12.cloned.1.call-done = bf16[32,3,640,80]{2,3,1,0:T(8,128)(2,1)} async-done(((bf16[16,3,640,80]{2,3,1,0:T(8,128)(2,1)}), bf16[32,3,640,80]{2,3,1,0:T(8,128)(2,1)}) %all-gather.12.cloned.1.call-update) | async-done | bytes 9830416 | tf_op jit(solution)/shard_map/all_gather | solution.py:98
  191.8 8.2 %fusion.38 = bf16[16,3,80,144,1]{2,3,1,0,4:T(8,128)(2,1)S(1)} fusion(bf16[2,16,3,640,80]{3,4,2,1,0:T(8,128)(2,1)} %bitcast.93, f32[144,2,640]{2,1,0:T(2,128)S(1)} %reshape.205, f32[2,640]{1,0:T(2,128)S(1)} %mul.106, f32[144]{0:T(256)S(1)} %rsqrt.21, f32[144]{0:T(256)S(1)} %div.35), kind=kOutput, calls=%fused_computation.53 | convolution fusion | flops 1416314880 | bytes 11679872 | tf_op jit(solution)/shard_map/pkc,kjmcd->mpjd/dot_general | solution.py:112
  200.1 1.7 copy.87
  201.8 5.7 %reshape.194 = bf16[3,1,16,9,1280]{4,0,3,2,1:T(4,128)(2,1)} reshape(bf16[3,144,16,80]{3,2,0,1:T(8,128)(2,1)} %copy.87) | data formatting | bytes 2211840 | tf_op jit(solution)/shard_map/reshape | solution.py:115
  207.5 9.0 %all-to-all-start.2 = ((bf16[3,1,16,9,1280]{4,0,3,1,2:T(4,128)(2,1)}), bf16[3,1,16,9,1280]{4,0,3,1,2:T(4,128)(2,1)S(1)}, u32[]{:S(2)}, u32[]{:S(2)}) async-start(bf16[3,1,16,9,1280]{4,0,3,1,2:T(4,128)(2,1)} %bitcast.85), calls=%async_computation.2 | async-start | bytes 2949120 | tf_op jit(solution)/shard_map/all_to_all | solution.py:119
  216.6 35.6 %all-to-all-done.2 = bf16[3,1,16,9,1280]{4,0,3,1,2:T(4,128)(2,1)S(1)} async-done(((bf16[3,1,16,9,1280]{4,0,3,1,2:T(4,128)(2,1)}), bf16[3,1,16,9,1280]{4,0,3,1,2:T(4,128)(2,1)S(1)}, u32[]{:S(2)}, u32[]{:S(2)}) %all-to-all-start.2) | async-done | bytes 1105952 | tf_op jit(solution)/shard_map/all_to_all | solution.py:119
  252.2 6.4 %slice_reduce_fusion.2 = (bf16[16,9,1280]{2,1,0:T(8,128)(2,1)S(1)}, bf16[16,9,1280]{2,1,0:T(8,128)(2,1)}, bf16[16,9,1280]{2,1,0:T(8,128)(2,1)}) fusion(bf16[3,1,16,9,1280]{4,0,3,1,2:T(4,128)(2,1)S(1)} %all-to-all-done.2), kind=kLoop, calls=%fused_computation.43 | loop fusion | bytes 2211840 | tf_op jit(solution)/shard_map/slice | solution.py:120
  258.5 1.8 reshape.227
  260.3 2.5 reshape.228
  262.8 1.6 reshape.226
  264.4 3.2 fusion.56
  267.5 2.1 fusion.26
  270.5 27.5 %all_to_all.35 = bf16[16,1,9,1280]{3,2,1,0:T(8,128)(2,1)S(1)} all-to-all(bf16[16,1,9,1280]{3,2,1,0:T(8,128)(2,1)S(1)} %reshape.229), channel_id=1, replica_groups=mesh['view'=16,'chip'=8,'core'=2] {'view'}, dimensions={0} | all-to-all | bytes 737280 | tf_op jit(solution)/shard_map/all_to_all | solution.py:34
  298.1 44.1 %all_to_all.36 = bf16[16,80,640]{2,1,0:T(8,128)(2,1)} all-to-all(bf16[16,80,640]{2,1,0:T(8,128)(2,1)S(1)} %stack.2), channel_id=1, replica_groups=mesh['view'=16,'chip'=8,'core'=2] {'view'}, dimensions={0} | all-to-all | bytes 3276800 | tf_op jit(solution)/shard_map/all_to_all | solution.py:118
  342.9 14.8 %all-gather.14.cloned.1.call-done = bf16[2560,640]{1,0:T(8,128)(2,1)} async-done(((bf16[1280,640]{1,0:T(8,128)(2,1)}), bf16[2560,640]{1,0:T(8,128)(2,1)}) %all-gather.14.cloned.1.call-update) | async-done | bytes 3276816 | tf_op jit(solution)/shard_map/all_gather | solution.py:122
  357.8 5.7 %copy.98 = bf16[2,640,1280]{2,1,0:T(8,128)(2,1)} copy(bf16[2,640,1280]{1,2,0:T(8,128)(2,1)} %bitcast.90) | data formatting | bytes 6553600 | tf_op jit(solution)/shard_map/pc,kcd->pkd/dot_general | solution.py:127
  363.5 3.9 %fusion.19 = bf16[1,1,2,72,1280]{4,3,2,1,0:T(8,128)(2,1)} fusion(f32[2,72,1280]{2,1,0:T(8,128)S(1)} %reshape.204, bf16[2,72,1280]{2,1,0:T(8,128)(2,1)S(1)} %dot_general.29, bf16[1280,1280,1]{1,0,2:T(8,128)(2,1)} %bitcast.80), kind=kOutput, calls=%fused_computation.24 | convolution fusion | flops 472227840 | bytes 4751360 | tf_op jit(solution)/shard_map/pc,kcd->pkd/dot_general | solution.py:127
  (72 shorter events, 10.8 us)
Async XLA Ops:
  6.5 87.7 %copy-start = (bf16[3,3,1280,80]{2,3,1,0:T(8,128)(2,1)S(1)}, bf16[3,3,1280,80]{2,3,1,0:T(8,128)(2,1)}, u32[]{:S(2)}) copy-start(bf16[3,3,1280,80]{2,3,1,0:T(8,128)(2,1)} %param.20) | copy-start | bytes 5529604
  6.5 50.4 %all-gather.8.cloned.1.call-start = ((), (), s32[]{:S(2)}) async-start(), calls=%async_computation.4 | async-start | bytes 6266880 | tf_op jit(solution)/shard_map/all_gather | solution.py:55
  7.3 154.9 %all-gather.10.cloned.1.call-start = ((), (), s32[]{:S(2)}) async-start(), calls=%async_computation.5 | async-start | bytes 5222400 | tf_op jit(solution)/shard_map/all_gather | solution.py:61
  58.7 133.1 %all-gather.12.cloned.1.call-start = ((), (), s32[]{:S(2)}) async-start(), calls=%async_computation.6 | async-start | bytes 14745600 | tf_op jit(solution)/shard_map/all_gather | solution.py:98
  61.2 13.4 %slice-start = ((s8[5898240]{0:T(1024)(128)(4,1)}), s8[1703936]{0:T(1024)(128)(4,1)S(1)}, s32[]{:S(2)}) async-start(s8[5898240]{0:T(1024)(128)(4,1)} %bitcast.77), calls=%async_computation.8 | async-start | bytes 3407872
  67.9 6.8 %slice-start.1 = ((s8[5898240]{0:T(1024)(128)(4,1)}), s8[4194304]{0:T(1024)(128)(4,1)S(1)}, s32[]{:S(2)}) async-start(s8[5898240]{0:T(1024)(128)(4,1)} %bitcast.77), calls=%async_computation.9 | async-start | bytes 8388608
  75.5 5.3 %copy-start.3 = (f32[1280]{0:T(1024)S(1)}, f32[1280]{0:T(1024)}, u32[]{:S(2)}) copy-start(f32[1280]{0:T(1024)} %get-tuple-element.26) | copy-start | bytes 15364
  75.5 5.3 %copy-start.4 = (f32[1280]{0:T(1024)S(1)}, f32[1280]{0:T(1024)}, u32[]{:S(2)}) copy-start(f32[1280]{0:T(1024)} %get-tuple-element.27) | copy-start | bytes 15364
  75.5 5.3 %copy-start.6 = (f32[1280]{0:T(1024)S(1)}, f32[1280]{0:T(1024)}, u32[]{:S(2)}) copy-start(f32[1280]{0:T(1024)} %param.15) | copy-start | bytes 15364
  75.5 5.3 %copy-start.7 = (f32[1280]{0:T(1024)S(1)}, f32[1280]{0:T(1024)}, u32[]{:S(2)}) copy-start(f32[1280]{0:T(1024)} %param.14) | copy-start | bytes 15364
  90.3 4.0 %copy-start.10 = (pred[8,10]{0,1:T(8,128)(4,1)S(1)}, pred[8,10]{0,1:T(8,128)(4,1)}, u32[]{:S(2)}) copy-start(pred[8,10]{0,1:T(8,128)(4,1)} %constant.46) | copy-start | bytes 244
  94.3 17.4 %copy-start.8 = (f32[80]{0:T(128)S(1)}, f32[80]{0:T(128)}, u32[]{:S(2)}) copy-start(f32[80]{0:T(128)} %dynamic_slice.14) | copy-start | bytes 964
  111.7 59.4 %copy-start.5 = (f32[1280]{0:T(1024)S(1)}, f32[1280]{0:T(1024)}, u32[]{:S(2)}) copy-start(f32[1280]{0:T(1024)} %param.22) | copy-start | bytes 15364
  111.7 59.5 %copy-start.2 = (bf16[80,1280]{1,0:T(8,128)(2,1)S(1)}, bf16[80,1280]{1,0:T(8,128)(2,1)}, u32[]{:S(2)}) copy-start(bf16[80,1280]{1,0:T(8,128)(2,1)} %param.24) | copy-start | bytes 614404
  163.2 17.9 %all-to-all-start = ((bf16[1,1,32,72,80]{4,3,1,0,2:T(8,128)(2,1)}), bf16[1,1,32,72,80]{4,3,1,0,2:T(8,128)(2,1)S(1)}, u32[]{:S(2)}, u32[]{:S(2)}) async-start(bf16[1,1,32,72,80]{4,3,1,0,2:T(8,128)(2,1)} %copy.83), calls=%async_computation | async-start | bytes 1179648 | tf_op jit(solution)/shard_map/all_to_all | solution.py:99
  200.1 16.4 %copy-start.9 = (f32[20]{0:T(128)S(1)}, f32[20]{0:T(128)}, u32[]{:S(2)}) copy-start(f32[20]{0:T(128)} %param.25) | copy-start | bytes 244
  207.5 44.7 %all-to-all-start.2 = ((bf16[3,1,16,9,1280]{4,0,3,1,2:T(4,128)(2,1)}), bf16[3,1,16,9,1280]{4,0,3,1,2:T(4,128)(2,1)S(1)}, u32[]{:S(2)}, u32[]{:S(2)}) async-start(bf16[3,1,16,9,1280]{4,0,3,1,2:T(4,128)(2,1)} %bitcast.85), calls=%async_computation.2 | async-start | bytes 2949120 | tf_op jit(solution)/shard_map/all_to_all | solution.py:119
  216.5 141.3 %all-gather.14.cloned.1.call-start = ((), (), s32[]{:S(2)}) async-start(), calls=%async_computation.7 | async-start | bytes 4915200 | tf_op jit(solution)/shard_map/all_gather | solution.py:122
  357.8 9.6 %copy-start.1 = (bf16[3,3,1280,80]{2,3,1,0:T(8,128)(2,1)S(1)}, bf16[3,3,1280,80]{2,3,1,0:T(8,128)(2,1)}, u32[]{:S(2)}) copy-start(bf16[3,3,1280,80]{2,3,1,0:T(8,128)(2,1)} %param.20) | copy-start | bytes 5529604
Sparse Core Ops, SparseCore 0:
  9.2 47.7 all-gather.7
  59.6 102.5 all-gather.9
  164.0 27.7 all-gather.11
  342.4 15.3 all-gather.13
